TPU v7x, 32 devices: a whole 2x2x4 slice. The times are simulated.
32 devices in a mesh: well: 4 (over y, x), tile: 8 (over z, core).
Axes of the slice: x: 2, y: 2, z: 4, core: 2. Of those that a mesh axis runs over, the one named last changes fastest.
Arguments:
- prior_state: float32 [3, 200, 8192], P(None, None, 'tile'), may hold values from -6 to 6
- pred_data: float32 [4096, 200], P(('well', 'tile')), may hold values from -6 to 6
- obs_pert: float32 [4096, 200], P(('well', 'tile')), may hold values from -12 to 12
- obs_std: float32 [4096], P(('well', 'tile')), may hold values from 0.5 to 2
- loc_mask: int32 [8, 32], P('tile', 'well'), may hold values from 0 to 1, as said below
- taper_level: int32 [8, 32], P('tile', 'well'), may hold values from 1 to 4
Outputs:
- analysis: float32 [3, 200, 8192], P(None, 'well', 'tile')
Inputs may be any that keep to these rules, and one draw needn't show every extreme that they name: `loc_mask`: each tile is localized to a set of data blocks whose size varies strongly from tile to tile; some tile is localized to most blocks.
All inputs are finite; a program needn't handle non-finite values.
Results may differ from a plain program's by a relative error of at most 0.0003.
Values sent between devices are 32-bit elements; how exact they have to be, the bound alone decides.
No kernel may reach another device: no remote copies, remote signals or barrier semaphores. Data moves between devices by JAX's collectives and lax.ppermute only.
A program may use at most 64 MiB of HBM per device.

v0:
```python
import jax
import jax.numpy as jnp
from jax import lax
from jax.sharding import PartitionSpec as P

BLOCK = 128


def chol_apply(system, right):
    factor = jnp.linalg.cholesky(system)
    middle = lax.linalg.triangular_solve(
        factor, right, left_side=True, lower=True, transpose_a=False
    )
    return lax.linalg.triangular_solve(factor, middle, left_side=True, lower=True, transpose_a=True)


def prepare(pred_rows, obs_rows, std_rows, norm_factor):
    data_anom = (pred_rows - jnp.mean(pred_rows, axis=1, keepdims=True)) * norm_factor
    innov = obs_rows - pred_rows
    row_weight = 1.0 / (4.0 * std_rows * std_rows)
    scaled = row_weight[:, None] * data_anom
    return (data_anom, innov, row_weight, scaled)


def shards(prior_state, pred_data, obs_pert, obs_std, loc_mask, taper_level):
    highest = lax.Precision.HIGHEST
    members = pred_data.shape[1]
    norm_factor = 1.0 / jnp.sqrt(jnp.float32(members - 1))
    data_anom, innov, row_weight, scaled = prepare(pred_data, obs_pert, obs_std, norm_factor)
    gram_matrix, cross_matrix = lax.psum(
        (
            jnp.dot(data_anom.T, scaled, precision=highest),
            jnp.dot(scaled.T, innov, precision=highest),
        ),
        ("well", "tile"),
    )
    system = jnp.eye(members, dtype=jnp.float32) + gram_matrix
    solved = chol_apply(system, cross_matrix)
    gain_rows = row_weight[:, None] * innov - jnp.dot(scaled, solved, precision=highest)
    group_anom, group_gain = (
        lax.all_gather(data_anom, "tile", axis=0, tiled=True),
        lax.all_gather(gain_rows, "tile", axis=0, tiled=True),
    )
    taper_row = loc_mask[0].astype(jnp.float32) * taper_level[0].astype(jnp.float32) / 4.0
    state_anom = (prior_state - jnp.mean(prior_state, axis=1, keepdims=True)) * norm_factor
    own_count = members // lax.axis_size("well")
    own_start = lax.axis_index("well") * own_count
    row_taper = jnp.repeat(taper_row, BLOCK)
    space = jnp.dot((group_anom * row_taper[:, None]).T, group_gain, precision=highest)
    space_mine = lax.psum_scatter(space, "well", scatter_dimension=1, tiled=True)
    increment = jnp.einsum("vnc,nm->vmc", state_anom, space_mine, precision=highest)
    prior_mine = lax.dynamic_slice_in_dim(prior_state, own_start, own_count, 1)
    return prior_mine + increment


def solution(mesh):
    return jax.shard_map(
        shards,
        mesh=mesh,
        in_specs=(
            P(None, None, "tile"),
            P(("well", "tile"), None),
            P(("well", "tile"), None),
            P(("well", "tile")),
            P("tile", "well"),
            P("tile", "well"),
        ),
        out_specs=P(None, "well", "tile"),
        check_vma=False,
    )
```

profile of v0, /device:TPU:4, one launch (start us, length us, event | category | flops | bytes accessed | tf_op | source)
XLA Modules:
  0.0 278.2 jit_solution(14750965140446197229)
XLA Ops:
  6.5 1.1 reduce_sum.18
  7.6 1.2 broadcast_multiply_fusion.1
  8.8 2.0 fusion.22
  10.8 2.0 fusion.21
  13.8 16.0 %all_gather.6 = f32[1024,200]{0,1:T(8,128)S(1)} all-gather(f32[128,200]{0,1:T(8,128)S(1)} %subtract_multiply_fusion.1), channel_id=1, replica_groups=mesh['well'=4,'tile'=8] {'tile'}, dimensions={0}, use_global_device_ids=true | all-gather | bytes 921600 | tf_op jit(solution)/shard_map/all_gather | solution.py:41
  30.6 110.1 %all-reduce.8.cloned.1.call-done = (f32[200,200]{1,0:T(8,128)}, f32[200,200]{0,1:T(8,128)}) async-done(((f32[200,200]{1,0:T(8,128)}, f32[200,200]{0,1:T(8,128)}), (f32[200,200]{1,0:T(8,128)}, f32[200,200]{0,1:T(8,128)})) %all-reduce.8.cloned.1.call-update) | async-done | bytes 320016 | tf_op jit(solution)/shard_map/psum | solution.py:30
  140.7 1.7 convert_add_fusion
  142.4 1.7 copy.10
  144.1 1.1 fusion.18
  146.5 13.2 %cholesky.51 = f32[128,128]{1,0:T(8,128)} custom-call(f32[128,128]{1,0:T(8,128)} %cholesky.124), custom_call_target="Cholesky" | custom-call | tf_op jit(solution)/shard_map/jit(cholesky)/cholesky | solution.py:10
  159.7 2.0 select_reduce_fusion
  161.7 1.5 cholesky.119
  163.2 11.3 %custom-call.16 = f32[1,128,128]{1,2,0:T(8,128)} custom-call(f32[1,128,128]{2,1,0:T(8,128)} %get-tuple-element.30), custom_call_target="InvertDiagBlocksLowerTriangular" | custom-call | tf_op jit(solution)/shard_map/jit(cholesky)/cholesky | solution.py:10
  174.5 1.7 constant_dynamic-update-slice_fusion.1
  176.2 1.6 convolution_subtract_fusion.3
  177.8 8.0 %cholesky.110 = f32[72,72]{1,0:T(8,128)} custom-call(f32[72,72]{1,0:T(8,128)} %convolution_subtract_fusion.3), custom_call_target="Cholesky" | custom-call | tf_op jit(solution)/shard_map/jit(cholesky)/cholesky | solution.py:10
  185.7 1.4 select_reduce_fusion.1
  187.8 1.3 compare_reduce_fusion.1
  190.3 1.0 select_select_fusion
  192.7 21.1 %custom-call.17 = f32[2,128,128]{1,2,0:T(8,128)} custom-call(f32[2,128,128]{2,1,0:T(8,128)} %pad_maximum_fusion), custom_call_target="InvertDiagBlocksLowerTriangular" | custom-call | tf_op jit(solution)/shard_map/triangular_solve | solution.py:14
  213.8 1.4 fusion.19
  215.2 1.2 convolution_subtract_fusion.2
  216.4 1.0 fusion.36
  217.4 1.0 fusion.35
  218.4 1.1 convolution_subtract_fusion
  219.6 1.2 fusion.26
  220.8 1.2 convolution_subtract_fusion.1
  222.0 17.3 %all_gather.7 = f32[1024,200]{0,1:T(8,128)S(1)} all-gather(f32[128,200]{0,1:T(8,128)S(1)} %convolution_subtract_fusion.1), channel_id=1, replica_groups=mesh['well'=4,'tile'=8] {'tile'}, dimensions={0}, use_global_device_ids=true | all-gather | bytes 921600 | tf_op jit(solution)/shard_map/all_gather | solution.py:42
  240.2 21.4 %fusion = f32[200,64]{0,1:T(8,128)S(1)} fusion(f32[200,200]{0,1:T(8,128)S(1)} %fusion.12), kind=kCustom, calls=%all-reduce-scatter | all-reduce-scatter fusion | flops 51201 | bytes 211712
  261.7 3.4 %collective-permute-start = (f32[200,42]{0,1:T(8,128)S(1)}, f32[200,42]{0,1:T(8,128)S(1)}, u32[]{:S(2)}, u32[]{:S(2)}) collective-permute-start(f32[200,42]{0,1:T(8,128)S(1)} %slice.74), channel_id=1, source_target_pairs={{0,8},{8,16},{16,24},{1,9},{9,17},{17,25},{2,10},{10,18},{18,26},{... | collective-permute-start | bytes 100808
  266.3 2.2 collective-permute-done
  268.7 2.6 fusion.7
  (39 shorter events, 6.8 us)
Async XLA Ops:
  6.5 23.3 %copy-start.9 = (s32[1,8]{1,0:T(1,128)S(1)}, s32[1,8]{1,0:T(1,128)}, u32[]{:S(2)}) copy-start(s32[1,8]{1,0:T(1,128)} %param.10) | copy-start | bytes 100
  6.5 23.3 %copy-start.8 = (s32[1,8]{1,0:T(1,128)S(1)}, s32[1,8]{1,0:T(1,128)}, u32[]{:S(2)}) copy-start(s32[1,8]{1,0:T(1,128)} %param.11) | copy-start | bytes 100
  6.5 23.3 %copy-start = (f32[3,200,1024]{2,1,0:T(8,128)S(1)}, f32[3,200,1024]{2,1,0:T(8,128)}, u32[]{:S(2)}) copy-start(f32[3,200,1024]{2,1,0:T(8,128)} %param.6) | copy-start | bytes 7372804
  6.5 134.2 %all-reduce.8.cloned.1.call-start = ((), (), s32[]{:S(2)}) async-start(), calls=%async_computation | async-start | bytes 819200 | tf_op jit(solution)/shard_map/psum | solution.py:30
  8.8 2.0 copy-start.6
  140.7 80.0 %copy-start.1 = (f32[128,200]{0,1:T(8,128)S(1)}, f32[128,200]{0,1:T(8,128)}, u32[]{:S(2)}) copy-start(f32[128,200]{0,1:T(8,128)} %param.7) | copy-start | bytes 307204
  140.7 80.0 %copy-start.4 = (f32[128,200]{0,1:T(8,128)S(1)}, f32[128,200]{0,1:T(8,128)}, u32[]{:S(2)}) copy-start(f32[128,200]{0,1:T(8,128)} %param.8) | copy-start | bytes 307204
  145.2 0.7 copy-start.3
  191.2 0.7 copy-start.2
  215.1 49.9 %copy-start.5 = (f32[3,1024]{1,0:T(4,128)S(1)}, f32[3,1024]{1,0:T(4,128)}, u32[]{:S(2)}) copy-start(f32[3,1024]{1,0:T(4,128)} %reduce_sum.19) | copy-start | bytes 36868
  215.1 49.9 %copy-start.7 = (u32[32]{0:T(128)S(1)}, u32[32]{0:T(128)}, u32[]{:S(2)}) copy-start(u32[32]{0:T(128)} %constant.155) | copy-start | bytes 388
  261.7 6.9 %collective-permute-start = (f32[200,42]{0,1:T(8,128)S(1)}, f32[200,42]{0,1:T(8,128)S(1)}, u32[]{:S(2)}, u32[]{:S(2)}) collective-permute-start(f32[200,42]{0,1:T(8,128)S(1)} %slice.74), channel_id=1, source_target_pairs={{0,8},{8,16},{16,24},{1,9},{9,17},{17,25},{2,10},{10,18},{18,26},{... | collective-permute-start | bytes 100808
Sparse Core Ops, SparseCore 0:
  13.0 127.6 all-reduce.7
where the time goes:
time: 279 us; the launch traced here: 278 us
  waiting for transfers between devices  112 us (40%)
  other arithmetic  67.3 us (24%)
  blocking collectives  54.7 us (20%)
  matrix products  19 us (7%)
  between operations  15.4 us (6%)
  local copies, waits for them, and re-layouts  6.12 us (2%)
  starting transfers between devices  3.37 us (1%)
    psum x1, waiting for transfers between devices, shards(): lax.psum((jnp.dot(data_anom.T, scaled, precision=highest), jnp.dot(scaled...  110 us
    another operation x7, other arithmetic, chol_apply(): factor = jnp.linalg.cholesky(system)  37.8 us
    another operation x6, other arithmetic, chol_apply(): lax.linalg.triangular_solve(factor, middle, left_side=True, lower=True, t...  22.8 us
    unnamed x1, blocking collectives  21.4 us
    all_gather x1, blocking collectives, shards(): lax.all_gather(gain_rows, 'tile', axis=0, tiled=True)  17.3 us
    all_gather x1, blocking collectives, shards(): lax.all_gather(data_anom, 'tile', axis=0, tiled=True)  16 us
  transfers between devices with their start and end apart: 2, of which 2 were waited for; matrix products, arithmetic and copies ran while one was open for 1% of the time, Pallas kernels for 0%

commit v1 on v0

--- a/solution.py
+++ b/solution.py
@@ -27,12 +27,15 @@
     members = pred_data.shape[1]
     norm_factor = 1.0 / jnp.sqrt(jnp.float32(members - 1))
     data_anom, innov, row_weight, scaled = prepare(pred_data, obs_pert, obs_std, norm_factor)
-    gram_matrix, cross_matrix = lax.psum(
-        (
-            jnp.dot(data_anom.T, scaled, precision=highest),
-            jnp.dot(scaled.T, innov, precision=highest),
+    gram_matrix, cross_matrix = jax.lax.psum(
+        jax.lax.psum(
+            (
+                jnp.dot(data_anom.T, scaled, precision=highest),
+                jnp.dot(scaled.T, innov, precision=highest),
+            ),
+            axis_name="tile",
         ),
-        ("well", "tile"),
+        axis_name="well",
     )
     system = jnp.eye(members, dtype=jnp.float32) + gram_matrix
     solved = chol_apply(system, cross_matrix)

time: 279 us -> 233 us (0.84)
  waiting for transfers between devices: 112 us -> 85.5 us
  other arithmetic: 67.3 us -> 56.5 us
  local copies, waits for them, and re-layouts: 6.12 us -> 1.22 us
  matrix products: 19 us -> 14.4 us
    psum x1 -> x2, waiting for transfers between devices: 110 us -> 83.2 us  [the longest x1 51.4 us: shards(): jax.lax.psum((jnp.dot(data_anom.T, scaled, precision=highest), jnp.dot(sc...]
    another operation x7, other arithmetic: 37.8 us -> 29.5 us  [chol_apply(): factor = jnp.linalg.cholesky(system)]
    another operation x2, matrix products: 3.27 us -> 0.42 us  [chol_apply(): factor = jnp.linalg.cholesky(system)]
    another operation x6, other arithmetic: 22.8 us -> 20 us  [chol_apply(): lax.linalg.triangular_solve(factor, middle, left_side=True, lower=True, t...]
  transfers between devices with their start and end apart: 2 -> 3, of which waited for: 2 -> 3; matrix products, arithmetic and copies ran while one was open for 1% -> 2% of each run, Pallas kernels for 0% -> 0%
where the time goes in v1:
time: 233 us; the launch traced here: 232 us
  waiting for transfers between devices  85.5 us (37%)
  other arithmetic  56.5 us (24%)
  blocking collectives  55.7 us (24%)
  between operations  15.6 us (7%)
  matrix products  14.4 us (6%)
  starting transfers between devices  3.42 us (1%)
    psum x1, waiting for transfers between devices, shards(): jax.lax.psum((jnp.dot(data_anom.T, scaled, precision=highest), jnp.dot(sc...  51.4 us
    psum x1, waiting for transfers between devices, shards(): jax.lax.psum(jax.lax.psum((jnp.dot(data_anom.T, scaled, precision=highest...  31.8 us
    another operation x7, other arithmetic, chol_apply(): factor = jnp.linalg.cholesky(system)  29.5 us
    unnamed x1, blocking collectives  22.8 us
    another operation x6, other arithmetic, chol_apply(): lax.linalg.triangular_solve(factor, middle, left_side=True, lower=True, t...  20 us
    all_gather x1, blocking collectives, shards(): lax.all_gather(data_anom, 'tile', axis=0, tiled=True)  17.3 us
    all_gather x1, blocking collectives, shards(): lax.all_gather(gain_rows, 'tile', axis=0, tiled=True)  15.6 us
  transfers between devices with their start and end apart: 3, of which 3 were waited for; matrix products, arithmetic and copies ran while one was open for 2% of the time, Pallas kernels for 0%

profile of v1, /device:TPU:4, one launch (start us, length us, event | category | flops | bytes accessed | tf_op | source)
XLA Modules:
  0.0 232.3 jit_solution(6956525697917233292)
XLA Ops:
  6.5 0.9 reduce_sum.18
  7.5 0.7 broadcast_multiply_fusion.1
  8.1 2.0 fusion.22
  10.1 2.0 fusion.21
  12.2 0.9 subtract_multiply_fusion.1
  13.1 0.7 multiply_bitcast_fusion
  13.9 1.8 reduce_sum.19
  15.8 51.4 %all-reduce.10.cloned.1.call-done = (f32[200,200]{1,0:T(8,128)}, f32[200,200]{0,1:T(8,128)}) async-done(((f32[200,200]{1,0:T(8,128)}, f32[200,200]{0,1:T(8,128)}), (f32[200,200]{1,0:T(8,128)}, f32[200,200]{0,1:T(8,128)})) %all-reduce.10.cloned.1.call-update) | async-done | bytes 320016 | tf_op jit(solution)/shard_map/psum | solution.py:31
  67.2 17.3 %all_gather.6 = f32[1024,200]{0,1:T(8,128)S(1)} all-gather(f32[128,200]{0,1:T(8,128)S(1)} %subtract_multiply_fusion.1), channel_id=1, replica_groups=mesh['well'=4,'tile'=8] {'tile'}, dimensions={0}, use_global_device_ids=true | all-gather | bytes 921600 | tf_op jit(solution)/shard_map/all_gather | solution.py:44
  84.5 31.8 %all-reduce.12.cloned.1.call-done = (f32[200,200]{1,0:T(8,128)}, f32[200,200]{0,1:T(8,128)}) async-done(((f32[200,200]{1,0:T(8,128)}, f32[200,200]{0,1:T(8,128)}), (f32[200,200]{1,0:T(8,128)}, f32[200,200]{0,1:T(8,128)})) %all-reduce.12.cloned.1.call-update) | async-done | bytes 320016 | tf_op jit(solution)/shard_map/psum | solution.py:30
  116.3 1.0 convert_add_fusion
  117.4 1.0 fusion.18
  118.4 11.7 %cholesky.51 = f32[128,128]{1,0:T(8,128)S(1)} custom-call(f32[128,128]{1,0:T(8,128)S(1)} %cholesky.124), custom_call_target="Cholesky" | custom-call | tf_op jit(solution)/shard_map/jit(cholesky)/cholesky | solution.py:10
  130.2 9.8 %custom-call.16 = f32[1,128,128]{1,2,0:T(8,128)S(1)} custom-call(f32[1,128,128]{2,1,0:T(8,128)S(1)} %get-tuple-element.32), custom_call_target="InvertDiagBlocksLowerTriangular" | custom-call | tf_op jit(solution)/shard_map/jit(cholesky)/cholesky | solution.py:10
  140.4 6.6 %cholesky.110 = f32[72,72]{1,0:T(8,128)S(1)} custom-call(f32[72,72]{1,0:T(8,128)S(1)} %convolution_subtract_fusion.3), custom_call_target="Cholesky" | custom-call | tf_op jit(solution)/shard_map/jit(cholesky)/cholesky | solution.py:10
  147.1 0.7 compare_reduce_fusion
  147.7 0.6 compare_reduce_fusion.1
  149.8 19.9 %custom-call.17 = f32[2,128,128]{1,2,0:T(8,128)S(1)} custom-call(f32[2,128,128]{2,1,0:T(8,128)S(1)} %pad_maximum_fusion), custom_call_target="InvertDiagBlocksLowerTriangular" | custom-call | tf_op jit(solution)/shard_map/triangular_solve | solution.py:14
  169.7 0.4 fusion.19
  170.3 0.3 convolution_subtract_fusion.2
  170.7 1.2 fusion.36
  171.9 1.0 fusion.35
  172.8 1.1 convolution_subtract_fusion
  174.0 1.2 fusion.26
  175.2 0.6 convolution_subtract_fusion.1
  175.8 15.6 %all_gather.7 = f32[1024,200]{0,1:T(8,128)S(1)} all-gather(f32[128,200]{0,1:T(8,128)S(1)} %convolution_subtract_fusion.1), channel_id=1, replica_groups=mesh['well'=4,'tile'=8] {'tile'}, dimensions={0}, use_global_device_ids=true | all-gather | bytes 921600 | tf_op jit(solution)/shard_map/all_gather | solution.py:45
  191.4 1.5 fusion.12
  192.9 22.8 %fusion = f32[200,64]{0,1:T(8,128)S(1)} fusion(f32[200,200]{0,1:T(8,128)} %fusion.12), kind=kCustom, calls=%all-reduce-scatter | all-reduce-scatter fusion | flops 51201 | bytes 211712
  215.8 3.4 %collective-permute-start = (f32[200,42]{0,1:T(8,128)S(1)}, f32[200,42]{0,1:T(8,128)S(1)}, u32[]{:S(2)}, u32[]{:S(2)}) collective-permute-start(f32[200,42]{0,1:T(8,128)S(1)} %slice.74), channel_id=1, source_target_pairs={{0,8},{8,16},{16,24},{1,9},{9,17},{17,25},{2,10},{10,18},{18,26},{... | collective-permute-start | bytes 100808
  219.2 0.6 dynamic-slice.8
  220.4 2.2 collective-permute-done
  222.9 2.6 %fusion.7 = f32[3,50,1024]{2,1,0:T(8,128)} fusion(f32[3,200,1024]{2,1,0:T(8,128)S(1)} %copy-done, f32[3,1024]{1,0:T(4,128)S(1)} %broadcast_multiply_fusion, s32[]{:T(128)S(6)} %select_n.7, f32[200,106]{0,1:T(8,128)S(1)} %concatenate.13, u32[]{:S(6)} %subtract.7), kind=kOutput, calls=%fused_computation.4 | convolution fusion | flops 370022400 | bytes 3833864 | tf_op jit(solution)/shard_map/vnc,nm->vmc/dot_general | solution.py:54
  (36 shorter events, 1.3 us)
Async XLA Ops:
  6.5 60.6 %all-reduce.10.cloned.1.call-start = ((), (), s32[]{:S(2)}) async-start(), calls=%async_computation | async-start | bytes 819200 | tf_op jit(solution)/shard_map/psum | solution.py:31
  12.2 104.1 %all-reduce.12.cloned.1.call-start = ((), (), s32[]{:S(2)}) async-start(), calls=%async_computation.1 | async-start | bytes 819200 | tf_op jit(solution)/shard_map/psum | solution.py:30
  116.3 53.4 %copy-start.5 = (f32[200,200]{1,0:T(8,128)S(1)}, f32[200,200]{1,0:T(8,128)}, u32[]{:S(2)}) copy-start(f32[200,200]{1,0:T(8,128)} %get-tuple-element.27) | copy-start | bytes 480004
  116.3 58.9 %copy-start.1 = (f32[128,200]{0,1:T(8,128)S(1)}, f32[128,200]{0,1:T(8,128)}, u32[]{:S(2)}) copy-start(f32[128,200]{0,1:T(8,128)} %param.7) | copy-start | bytes 307204
  116.3 58.9 %copy-start.3 = (f32[128,200]{0,1:T(8,128)S(1)}, f32[128,200]{0,1:T(8,128)}, u32[]{:S(2)}) copy-start(f32[128,200]{0,1:T(8,128)} %param.8) | copy-start | bytes 307204
  149.7 20.5 %copy-start.2 = (f32[200,200]{1,0:T(8,128)}, f32[200,200]{1,0:T(8,128)S(1)}, u32[]{:S(2)}) copy-start(f32[200,200]{1,0:T(8,128)S(1)} %select_select_fusion) | copy-start | bytes 480004
  169.7 0.7 copy-start.4
  170.3 48.8 %copy-start.6 = (u32[32]{0:T(128)S(1)}, u32[32]{0:T(128)}, u32[]{:S(2)}) copy-start(u32[32]{0:T(128)} %constant.155) | copy-start | bytes 388
  170.7 52.2 %copy-start = (f32[3,200,1024]{2,1,0:T(8,128)S(1)}, f32[3,200,1024]{2,1,0:T(8,128)}, u32[]{:S(2)}) copy-start(f32[3,200,1024]{2,1,0:T(8,128)} %param.6) | copy-start | bytes 7372804
  215.8 6.9 %collective-permute-start = (f32[200,42]{0,1:T(8,128)S(1)}, f32[200,42]{0,1:T(8,128)S(1)}, u32[]{:S(2)}, u32[]{:S(2)}) collective-permute-start(f32[200,42]{0,1:T(8,128)S(1)} %slice.74), channel_id=1, source_target_pairs={{0,8},{8,16},{16,24},{1,9},{9,17},{17,25},{2,10},{10,18},{18,26},{... | collective-permute-start | bytes 100808
Sparse Core Ops, SparseCore 0:
  12.3 54.8 all-reduce.9
  70.5 45.7 all-reduce.11
